TPU v7x, 512 devices: a whole 4x8x8 slice. The times are simulated.
512 devices in a mesh: dp: 64 (over z, x, core), mp: 8 (over y).
Axes of the slice: x: 4, y: 8, z: 8, core: 2. Of those that a mesh axis runs over, the one named last changes fastest.
Arguments:
- micro_grads: bfloat16 [64, 2, 768, 768], P('dp', None, None, 'mp'), may hold values from -16 to 16
- master: float32 [768, 768], P('dp', 'mp'), may hold values from -0.21875 to 0.21875
- moment: float32 [768, 768], P('dp', 'mp'), may hold values from -1.5 to 1.5
- second: float32 [768, 768], P('dp', 'mp'), may hold values from 0.001 to 0.1
- left_basis: float32 [768, 768], P(None, 'dp'), may hold values from -0.21875 to 0.21875
- right_basis: float32 [768, 768], P(None, 'mp'), may hold values from -0.21875 to 0.21875
- left_stat: float32 [768, 768], P('mp'), may hold values from -2 to 5, as said below
- right_stat: float32 [768, 768], P('mp'), may hold values from -2 to 5, as said below
Outputs:
- weights_block: bfloat16 [768, 768], P(None, 'mp')
- new_master: float32 [768, 768], P('dp', 'mp')
- new_moment: float32 [768, 768], P('dp', 'mp')
- new_second: float32 [768, 768], P('dp', 'mp')
- new_left_stat: float32 [768, 768], P('mp')
- new_right_stat: float32 [768, 768], P('mp')
- new_left_basis: float32 [768, 768], P('mp')
- new_right_basis: float32 [768, 768], P('mp')
Inputs may be any that keep to these rules, and one draw needn't show every extreme that they name: `left_stat`: symmetric. `right_stat`: symmetric.
All inputs are finite; a program needn't handle non-finite values.
Results may differ from a plain program's by a relative error of at most 0.004.
The roundings to bfloat16 on the way count: a program that leaves them out, or rounds other values in their place, can miss the bound.
Values may be sent and summed in bfloat16 or wider, within the bound.
No kernel may reach another device: no remote copies, remote signals or barrier semaphores. Data moves between devices by JAX's collectives and lax.ppermute only.
A program may use at most 64 MiB of HBM per device.

v0:
```python
import jax
import jax.numpy as jnp
from jax import lax
from jax.sharding import PartitionSpec as P

beta_one = 0.9
beta_two = 0.95
beta_stat = 0.95
learn_rate = 0.02
adam_eps = 1e-08
norm_eps = 1e-06
quint_a = 1.875
quint_b = -1.25
quint_c = 0.375
highest = lax.Precision.HIGHEST


def for_sending(x):

    def short(part):
        return part.astype(jnp.bfloat16) if part.dtype == jnp.float32 else part

    return jax.tree.map(short, x)


def all_rows(pair):
    return jax.tree.map(
        lambda part, own: part.astype(own.dtype),
        lax.all_gather(for_sending(pair), "mp", axis=0, tiled=True),
        pair,
    )


def row_gram(row_part, whole_part):
    return lax.dot_general(
        row_part, whole_part, (((1,), (1,)), ((), ())), preferred_element_type=jnp.float32
    )


def scatter_sum(x, axis):
    count = lax.axis_size(axis)
    chunks = x.reshape((count, x.shape[0] // count) + x.shape[1:])
    return jnp.sum(lax.all_to_all(chunks, axis, 0, 0, tiled=False), axis=0)


def gather_rows(x, axis):
    count = lax.axis_size(axis)
    return lax.all_to_all(jnp.broadcast_to(x[None], (count,) + x.shape), axis, 0, 0, tiled=False)


def per_device(micro_grads, master, moment, second, left_basis, right_basis, left_stat, right_stat):
    dp_count = lax.axis_size("dp")
    micro_count = micro_grads.shape[1]
    local_sum = jnp.sum(micro_grads[0], axis=0, dtype=jnp.float32)
    grad_piece = scatter_sum(local_sum, "dp") / (micro_count * dp_count)
    new_moment = beta_one * moment + (1.0 - beta_one) * grad_piece
    pieces = gather_rows(jnp.stack([grad_piece, new_moment]), "dp")
    pieces = jnp.swapaxes(pieces, 0, 1).reshape(2, -1, pieces.shape[-1])
    left_full = lax.all_gather(left_basis, "dp", axis=1, tiled=True)
    both_full = lax.all_gather(pieces, "mp", axis=2, tiled=True)
    right_full = lax.all_gather(right_basis, "mp", axis=1, tiled=True)
    grad_full = both_full[0]
    moment_full = both_full[1]

    def rotate(matrix):
        left_part = lax.dot_general(left_basis, matrix, (((0,), (0,)), ((), ())), precision=highest)
        return jnp.dot(left_part, right_basis, precision=highest)

    rot_grad = rotate(grad_full)
    rot_moment = rotate(moment_full)
    new_second = beta_two * second + (1.0 - beta_two) * rot_grad * rot_grad
    rot_step = rot_moment / (jnp.sqrt(new_second) + adam_eps)
    back_half = scatter_sum(
        lax.dot_general(right_basis, rot_step, (((1,), (1,)), ((), ())), precision=highest), "mp"
    )
    step_piece = scatter_sum(
        lax.dot_general(left_basis, back_half, (((1,), (1,)), ((), ())), precision=highest), "dp"
    )
    new_master = master - learn_rate * step_piece
    weights_block = gather_rows(new_master.astype(jnp.bfloat16), "dp").reshape(
        -1, new_master.shape[1]
    )
    band_width = right_basis.shape[1]
    band_start = lax.axis_index("mp") * band_width
    grad_band = lax.dynamic_slice_in_dim(grad_full, band_start, band_width, 0)
    grad_strip = lax.dynamic_slice_in_dim(grad_full, band_start, band_width, 1)
    left_outer = lax.dot_general(grad_band, grad_full, (((1,), (1,)), ((), ())), precision=highest)
    right_outer = lax.dot_general(
        grad_strip, grad_full, (((0,), (0,)), ((), ())), precision=highest
    )
    new_left_stat = beta_stat * left_stat + (1.0 - beta_stat) * left_outer
    new_right_stat = beta_stat * right_stat + (1.0 - beta_stat) * right_outer
    order_count = left_stat.shape[1]
    power_left = jnp.dot(
        new_left_stat.astype(jnp.bfloat16),
        left_full.astype(jnp.bfloat16),
        preferred_element_type=jnp.float32,
    )
    power_right = jnp.dot(
        new_right_stat.astype(jnp.bfloat16),
        right_full.astype(jnp.bfloat16),
        preferred_element_type=jnp.float32,
    )
    total_left, total_right = lax.psum(
        (jnp.sum(power_left * power_left), jnp.sum(power_right * power_right)), "mp"
    )
    start_left = lax.optimization_barrier(
        (power_left * lax.rsqrt(total_left * (4.0 / order_count) + norm_eps)).astype(jnp.bfloat16)
    )
    start_right = lax.optimization_barrier(
        (power_right * lax.rsqrt(total_right * (4.0 / order_count) + norm_eps)).astype(jnp.bfloat16)
    )
    start_rows = (start_left, start_right)
    start_whole = all_rows(start_rows)
    gram_rows = tuple(
        (
            lax.optimization_barrier(row_gram(row_part, whole_part).astype(jnp.bfloat16))
            for row_part, whole_part in zip(start_rows, start_whole)
        )
    )
    gram_whole = all_rows(gram_rows)
    middle_rows = []
    for row_part, gram_part, gram_all, whole_part in zip(
        start_rows, gram_rows, gram_whole, start_whole
    ):
        square = jnp.dot(gram_part, gram_all, preferred_element_type=jnp.float32)
        poly_rows = (quint_b * gram_part.astype(jnp.float32) + quint_c * square).astype(
            jnp.bfloat16
        )
        middle = quint_a * row_part.astype(jnp.float32) + jnp.dot(
            poly_rows, whole_part, preferred_element_type=jnp.float32
        )
        middle_rows.append(lax.optimization_barrier(middle.astype(jnp.bfloat16)))
    middle_whole = all_rows(tuple(middle_rows))
    new_bases = []
    for row_part, whole_part in zip(middle_rows, middle_whole):
        gram_two = row_gram(row_part, whole_part).astype(jnp.bfloat16)
        new_bases.append(
            1.5 * row_part.astype(jnp.float32)
            - 0.5 * jnp.dot(gram_two, whole_part, preferred_element_type=jnp.float32)
        )
    return (
        weights_block,
        new_master,
        new_moment,
        new_second,
        new_left_stat,
        new_right_stat,
        new_bases[0],
        new_bases[1],
    )


def solution(mesh):
    in_specs = (
        P("dp", None, None, "mp"),
        P("dp", "mp"),
        P("dp", "mp"),
        P("dp", "mp"),
        P(None, "dp"),
        P(None, "mp"),
        P("mp", None),
        P("mp", None),
    )
    out_specs = (
        P(None, "mp"),
        P("dp", "mp"),
        P("dp", "mp"),
        P("dp", "mp"),
        P("mp", None),
        P("mp", None),
        P("mp", None),
        P("mp", None),
    )
    return jax.shard_map(
        per_device, mesh=mesh, in_specs=in_specs, out_specs=out_specs, check_vma=False
    )
```

profile of v0, /device:TPU:2, one launch (start us, length us, event | category | flops | bytes accessed | tf_op | source)
XLA Modules:
  0.0 490.6 jit_solution(16406727266121706216)
XLA Ops:
  7.2 1.4 bitcast_convert_fusion
  8.7 1.0 convert_reduce_fusion
  9.7 0.2 copy.20
  10.0 31.4 %all_to_all.25 = f32[64,12,96]{2,1,0:T(8,128)S(1)} all-to-all(f32[64,12,96]{2,1,0:T(8,128)S(1)} %reshape.45), channel_id=1, replica_groups=mesh['dp'=64,'mp'=8] {'dp'}, dimensions={0} | all-to-all | bytes 589824 | tf_op jit(solution)/shard_map/all_to_all | solution.py:43
  41.3 0.1 reduce_sum.55
  41.5 0.2 broadcast_in_dim.4
  41.7 28.9 %all_to_all.26 = f32[64,2,12,96]{3,1,2,0:T(2,128)S(1)} all-to-all(f32[64,2,12,96]{3,1,2,0:T(2,128)S(1)} %broadcast_in_dim.4), channel_id=1, replica_groups=mesh['dp'=64,'mp'=8] {'dp'}, dimensions={0} | all-to-all | bytes 1179648 | tf_op jit(solution)/shard_map/all_to_all | solution.py:48
  70.6 1.2 copy.22
  71.8 0.7 convert.1
  72.5 0.2 all-gather.21.cloned.1.call-start
  72.7 27.0 %all-gather.27.cloned.1.call-done = bf16[64,12,768]{2,1,0:T(8,128)(2,1)} async-done(((bf16[1,12,768]{2,1,0:T(8,128)(2,1)}), bf16[64,12,768]{2,1,0:T(8,128)(2,1)}) %all-gather.27.cloned.1.call-update) | async-done | bytes 1179664 | tf_op jit(solution)/shard_map/all_gather | solution.py:59
  99.7 3.1 reshape.52
  102.9 59.1 %all-gather.11.cloned.1.call-done = f32[2,768,768]{1,0,2:T(2,128)} async-done(((f32[2,768,96]{1,0,2:T(2,128)}), f32[2,768,768]{1,0,2:T(2,128)}) %all-gather.11.cloned.1.call-update) | async-done | bytes 4718608 | tf_op jit(solution)/shard_map/all_gather | solution.py:60
  162.0 9.3 %fusion.53 = (f32[1,768,768]{1,0,2:T(1,128)S(1)}, f32[1,768,768]{1,0,2:T(1,128)}) fusion(f32[2,768,768]{1,0,2:T(2,128)} %all-gather.11.cloned.1.call-done), kind=kLoop, calls=%fused_computation.70 | loop fusion | bytes 9437184 | tf_op jit(solution)/shard_map/slice | solution.py:62
  171.4 0.9 constant_dynamic-slice_fusion.1
  172.3 1.5 fusion.23
  173.8 1.8 multiply_reduce_fusion.1
  175.7 2.4 fusion.20
  178.1 27.0 %all-gather.19.cloned.1.call-done = bf16[768,768]{0,1:T(8,128)(2,1)} async-done(((bf16[768,96]{0,1:T(8,128)(2,1)}), bf16[768,768]{0,1:T(8,128)(2,1)}) %all-gather.19.cloned.1.call-update) | async-done | bytes 1179664 | tf_op jit(solution)/shard_map/all_gather | solution.py:61
  205.1 2.4 multiply_reduce_fusion
  207.5 16.5 %all-reduce = (f32[]{:T(128)}, f32[]{:T(128)}) all-reduce(f32[]{:T(128)} %get-tuple-element.32, f32[]{:T(128)} %get-tuple-element.34), channel_id=1, replica_groups=mesh['dp'=64,'mp'=8] {'mp'}, use_global_device_ids=true, to_apply=%region_5.0 | all-reduce | flops 2 | bytes 16 | tf_op jit(solution)/shard_map/psum | solution.py:104
  224.8 0.7 multiply_convert_fusion
  226.2 0.7 multiply_convert_fusion.1
  227.0 39.7 %all-gather.21.cloned.1.call-done = bf16[768,768]{1,0:T(8,128)(2,1)} async-done(((bf16[96,768]{1,0:T(8,128)(2,1)}), bf16[768,768]{1,0:T(8,128)(2,1)}) %all-gather.21.cloned.1.call-update) | async-done | bytes 1179664 | tf_op jit(solution)/shard_map/all_gather | solution.py:29
  266.7 2.5 convolution_convert_fusion.1
  269.3 40.1 %all-gather.13.cloned.1.call-done = bf16[768,768]{1,0:T(8,128)(2,1)} async-done(((bf16[96,768]{1,0:T(8,128)(2,1)}), bf16[768,768]{1,0:T(8,128)(2,1)}) %all-gather.13.cloned.1.call-update) | async-done | bytes 1179664 | tf_op jit(solution)/shard_map/all_gather | solution.py:29
  309.5 2.4 convolution_convert_fusion.3
  312.0 40.2 %all-gather.23.cloned.1.call-done = bf16[768,768]{1,0:T(8,128)(2,1)} async-done(((bf16[96,768]{1,0:T(8,128)(2,1)}), bf16[768,768]{1,0:T(8,128)(2,1)}) %all-gather.23.cloned.1.call-update) | async-done | bytes 1179664 | tf_op jit(solution)/shard_map/all_gather | solution.py:29
  352.2 2.9 fusion.33
  355.2 0.3 all-gather.17.cloned.1.call-start
  355.5 2.0 fusion.4
  357.5 0.3 fusion.47
  357.9 2.0 fusion.6
  359.9 35.2 %all-gather.15.cloned.1.call-done = bf16[768,768]{1,0:T(8,128)(2,1)} async-done(((bf16[96,768]{1,0:T(8,128)(2,1)}), bf16[768,768]{1,0:T(8,128)(2,1)}) %all-gather.15.cloned.1.call-update) | async-done | bytes 1179664 | tf_op jit(solution)/shard_map/all_gather | solution.py:29
  395.1 2.5 fusion.31
  397.7 0.3 convolution_divide_fusion
  398.0 0.3 convolution_bitcast_fusion.1
  398.4 12.5 %all_to_all.27 = f32[8,96,12]{1,2,0:T(8,128)S(1)} all-to-all(f32[8,96,12]{1,2,0:T(8,128)S(1)} %copy.23), channel_id=1, replica_groups=mesh['dp'=64,'mp'=8] {'mp'}, dimensions={0} | all-to-all | bytes 73728 | tf_op jit(solution)/shard_map/all_to_all | solution.py:43
  410.9 0.4 convolution_bitcast_fusion
  411.4 0.2 copy.25
  411.6 28.3 %all_to_all.28 = f32[64,12,96]{2,1,0:T(8,128)S(1)} all-to-all(f32[64,12,96]{2,1,0:T(8,128)S(1)} %reshape.48), channel_id=1, replica_groups=mesh['dp'=64,'mp'=8] {'dp'}, dimensions={0} | all-to-all | bytes 589824 | tf_op jit(solution)/shard_map/all_to_all | solution.py:43
  439.9 0.6 fusion.52
  440.6 17.9 %all_to_all.29 = bf16[64,12,96]{2,1,0:T(8,128)(2,1)S(1)} all-to-all(bf16[64,12,96]{2,1,0:T(8,128)(2,1)S(1)} %broadcast_in_dim.5), channel_id=1, replica_groups=mesh['dp'=64,'mp'=8] {'dp'}, dimensions={0} | all-to-all | bytes 294912 | tf_op jit(solution)/shard_map/all_to_all | solution.py:48
  458.5 0.1 reshape.49
  458.6 0.8 copy.26
  459.4 3.1 fusion.26
  462.5 18.4 %all-gather.17.cloned.1.call-done = bf16[768,768]{1,0:T(8,128)(2,1)} async-done(((bf16[96,768]{1,0:T(8,128)(2,1)}), bf16[768,768]{1,0:T(8,128)(2,1)}) %all-gather.17.cloned.1.call-update) | async-done | bytes 1179664 | tf_op jit(solution)/shard_map/all_gather | solution.py:29
  480.9 3.1 fusion.28
  (70 shorter events, 1.0 us)
Async XLA Ops:
  7.2 92.6 %all-gather.27.cloned.1.call-start = ((), (), s32[]{:S(2)}) async-start(), calls=%async_computation.13 | async-start | bytes 1597440 | tf_op jit(solution)/shard_map/all_gather | solution.py:59
  8.6 153.4 %all-gather.11.cloned.1.call-start = ((), (), s32[]{:S(2)}) async-start(), calls=%async_computation.5 | async-start | bytes 5308416 | tf_op jit(solution)/shard_map/all_gather | solution.py:60
  9.9 31.5 %copy-start.20 = (f32[12,96]{1,0:T(8,128)S(1)}, f32[12,96]{1,0:T(8,128)}, u32[]{:S(2)}) copy-start(f32[12,96]{1,0:T(8,128)} %param.10) | copy-start | bytes 13828
  41.4 29.1 %copy-start.17 = (f32[12,96]{1,0:T(8,128)}, f32[12,96]{1,0:T(8,128)S(1)}, u32[]{:S(2)}) copy-start(f32[12,96]{1,0:T(8,128)S(1)} %get-tuple-element.31) | copy-start | bytes 13828
  70.6 1.2 copy-start.1
  71.7 133.4 %all-gather.19.cloned.1.call-start = ((), (), s32[]{:S(2)}) async-start(), calls=%async_computation.9 | async-start | bytes 1327104 | tf_op jit(solution)/shard_map/all_gather | solution.py:61
  72.5 194.2 %all-gather.21.cloned.1.call-start = ((), (), s32[]{:S(2)}) async-start(), calls=%async_computation.10 | async-start | bytes 1327104 | tf_op jit(solution)/shard_map/all_gather | solution.py:29
  171.3 1.0 copy-start.14
  172.3 1.6 copy-start.3
  173.8 4.2 copy-start.10
  173.8 1.8 copy-start.15
  178.1 47.4 %copy-start.11 = (f32[96,768]{1,0:T(8,128)}, f32[96,768]{1,0:T(8,128)S(1)}, u32[]{:S(2)}) copy-start(f32[96,768]{1,0:T(8,128)S(1)} %fusion.20) | copy-start | bytes 884740
  205.1 21.1 %copy-start.12 = (f32[96,768]{1,0:T(8,128)S(1)}, f32[96,768]{1,0:T(8,128)}, u32[]{:S(2)}) copy-start(f32[96,768]{1,0:T(8,128)} %get-tuple-element.33) | copy-start | bytes 884740
  225.5 84.0 %all-gather.13.cloned.1.call-start = ((), (), s32[]{:S(2)}) async-start(), calls=%async_computation.6 | async-start | bytes 1327104 | tf_op jit(solution)/shard_map/all_gather | solution.py:29
  226.9 82.6 %copy-start.4 = (bf16[96,768]{1,0:T(8,128)(2,1)S(1)}, bf16[96,768]{1,0:T(8,128)(2,1)}, u32[]{:S(2)}) copy-start(bf16[96,768]{1,0:T(8,128)(2,1)} %multiply_convert_fusion.1) | copy-start | bytes 442372
  226.9 125.3 %all-gather.23.cloned.1.call-start = ((), (), s32[]{:S(2)}) async-start(), calls=%async_computation.11 | async-start | bytes 1327104 | tf_op jit(solution)/shard_map/all_gather | solution.py:29
  269.2 83.0 %copy-start.5 = (bf16[96,768]{1,0:T(8,128)(2,1)S(1)}, bf16[96,768]{1,0:T(8,128)(2,1)}, u32[]{:S(2)}) copy-start(bf16[96,768]{1,0:T(8,128)(2,1)} %multiply_convert_fusion) | copy-start | bytes 442372
  269.3 83.0 %copy-start.9 = (bf16[96,768]{1,0:T(8,128)(2,1)S(1)}, bf16[96,768]{1,0:T(8,128)(2,1)}, u32[]{:S(2)}) copy-start(bf16[96,768]{1,0:T(8,128)(2,1)} %convolution_convert_fusion.1) | copy-start | bytes 442372
  269.3 125.9 %all-gather.15.cloned.1.call-start = ((), (), s32[]{:S(2)}) async-start(), calls=%async_computation.7 | async-start | bytes 1327104 | tf_op jit(solution)/shard_map/all_gather | solution.py:29
  311.9 43.5 %copy-start.13 = (f32[768,12]{0,1:T(8,128)S(1)}, f32[768,12]{0,1:T(8,128)}, u32[]{:S(2)}) copy-start(f32[768,12]{0,1:T(8,128)} %param.12) | copy-start | bytes 110596
  312.0 147.4 %all-gather.25.cloned.1.call-start = ((), (), s32[]{:S(2)}) async-start(), calls=%async_computation.12 | async-start | bytes 1327104 | tf_op jit(solution)/shard_map/all_gather | solution.py:29
  355.2 2.4 copy-start.18
  355.2 125.8 %all-gather.17.cloned.1.call-start = ((), (), s32[]{:S(2)}) async-start(), calls=%async_computation.8 | async-start | bytes 1327104 | tf_op jit(solution)/shard_map/all_gather | solution.py:29
  355.4 2.4 copy-start
  357.8 39.9 %copy-start.16 = (f32[12,96]{1,0:T(8,128)}, f32[12,96]{1,0:T(8,128)S(1)}, u32[]{:S(2)}) copy-start(f32[12,96]{1,0:T(8,128)S(1)} %fusion.47) | copy-start | bytes 13828
  357.9 37.3 %copy-start.2 = (bf16[768,768]{1,0:T(8,128)(2,1)S(1)}, bf16[768,768]{1,0:T(8,128)(2,1)}, u32[]{:S(2)}) copy-start(bf16[768,768]{1,0:T(8,128)(2,1)} %all-gather.13.cloned.1.call-done) | copy-start | bytes 3538948
  357.9 37.2 %copy-start.8 = (bf16[96,768]{1,0:T(8,128)(2,1)S(1)}, bf16[96,768]{1,0:T(8,128)(2,1)}, u32[]{:S(2)}) copy-start(bf16[96,768]{1,0:T(8,128)(2,1)} %convolution_convert_fusion.3) | copy-start | bytes 442372
  411.5 28.4 %copy-start.19 = (f32[12,96]{1,0:T(8,128)S(1)}, f32[12,96]{1,0:T(8,128)}, u32[]{:S(2)}) copy-start(f32[12,96]{1,0:T(8,128)} %param.9) | copy-start | bytes 13828
  439.8 19.5 %copy-start.6 = (bf16[96,768]{1,0:T(8,128)(2,1)S(1)}, bf16[96,768]{1,0:T(8,128)(2,1)}, u32[]{:S(2)}) copy-start(bf16[96,768]{1,0:T(8,128)(2,1)} %fusion.33) | copy-start | bytes 442372
  459.4 21.5 %copy-start.7 = (bf16[96,768]{1,0:T(8,128)(2,1)S(1)}, bf16[96,768]{1,0:T(8,128)(2,1)}, u32[]{:S(2)}) copy-start(bf16[96,768]{1,0:T(8,128)(2,1)} %fusion.31) | copy-start | bytes 442372
Sparse Core Ops, SparseCore 0:
  11.9 87.7 all-gather.26
  101.8 60.1 all-gather.10
  164.7 40.3 all-gather.18
  225.6 41.0 all-gather.20
  269.2 40.2 all-gather.12
  312.0 40.2 all-gather.22
  354.9 40.2 all-gather.14
  397.8 40.2 all-gather.24
  440.7 40.1 all-gather.16
where the time goes:
time: 491 us
  waiting for transfers between devices  287 us (58%)
  blocking collectives  135 us (27%)
  matrix products  30.2 us (6%)
  local copies, waits for them, and re-layouts  16.3 us (3%)
  between operations  15.6 us (3%)
  other arithmetic  5.29 us (1%)
    all_gather x6, waiting for transfers between devices, all_rows(): lax.all_gather(for_sending(pair), 'mp', axis=0, tiled=True)  174 us
    all_to_all x3, blocking collectives, scatter_sum(): return jnp.sum(lax.all_to_all(chunks, axis, 0, 0, tiled=False), axis=0)  72.1 us
    all_gather x1, waiting for transfers between devices, per_device(): both_full = lax.all_gather(pieces, 'mp', axis=2, tiled=True)  59.1 us
    all_to_all x2, blocking collectives, gather_rows(): lax.all_to_all(jnp.broadcast_to(x[None], (count,) + x.shape), axis, 0, 0,...  46.8 us
    all_gather x1, waiting for transfers between devices, per_device(): right_full = lax.all_gather(right_basis, 'mp', axis=1, tiled=True)  27 us
    all_gather x1, waiting for transfers between devices, per_device(): left_full = lax.all_gather(left_basis, 'dp', axis=1, tiled=True)  27 us
    psum x1, blocking collectives, per_device(): lax.psum((jnp.sum(power_left * power_left), jnp.sum(power_right * power_r...  16.5 us
  transfers between devices with their start and end apart: 9, of which 8 were waited for; matrix products, arithmetic and copies ran while one was open for 9% of the time, Pallas kernels for 0%

commit v1 on v0

--- a/solution.py
+++ b/solution.py
@@ -58,7 +58,12 @@
     pieces = jnp.swapaxes(pieces, 0, 1).reshape(2, -1, pieces.shape[-1])
     left_full = lax.all_gather(left_basis, "dp", axis=1, tiled=True)
     both_full = lax.all_gather(pieces, "mp", axis=2, tiled=True)
-    right_full = lax.all_gather(right_basis, "mp", axis=1, tiled=True)
+    ring = [right_basis]
+    for hop in range(7):
+        ring.append(lax.ppermute(ring[-1], "mp", [(dev, (dev + 1) % 8) for dev in range(8)]))
+    right_full = jnp.roll(
+        jnp.concatenate(ring[::-1], axis=1), (lax.axis_index("mp") + 1) * ring[0].shape[1], axis=1
+    )
     grad_full = both_full[0]
     moment_full = both_full[1]
 

time: 491 us -> 466 us (0.949)
  waiting for transfers between devices: 287 us -> 236 us
  starting transfers between devices: 0.77 us -> 15.6 us
  local copies, waits for them, and re-layouts: 16.3 us -> 27.1 us
    ppermute x0 -> x7, waiting for transfers between devices: none -> 50.7 us  [per_device(): lax.ppermute(ring[-1], 'mp', [(dev, (dev + 1) % 8) for dev in range(8)])]
    all_gather x1, waiting for transfers between devices: 59.1 us -> 15.1 us  [per_device(): both_full = lax.all_gather(pieces, 'mp', axis=2, tiled=True)]
    all_gather x1 -> x0, waiting for transfers between devices: 27 us -> none  [per_device(): right_full = lax.all_gather(right_basis, 'mp', axis=1, tiled=True)]
    all_gather x1, waiting for transfers between devices: 27 us -> 0.01 us  [per_device(): left_full = lax.all_gather(left_basis, 'dp', axis=1, tiled=True)]
    ppermute x0 -> x7, starting transfers between devices: none -> 15.1 us  [per_device(): lax.ppermute(ring[-1], 'mp', [(dev, (dev + 1) % 8) for dev in range(8)])]
    unnamed x43 -> x54, local copies, waits for them, and re-layouts: 0.96 us -> 11 us
  transfers between devices with their start and end apart: 9 -> 15, of which waited for: 8 -> 13; matrix products, arithmetic and copies ran while one was open for 9% -> 8% of each run, Pallas kernels for 0% -> 0%
where the time goes in v1:
time: 466 us; the launch traced here: 465 us
  waiting for transfers between devices  236 us (51%)
  blocking collectives  135 us (29%)
  matrix products  30.3 us (7%)
  local copies, waits for them, and re-layouts  27.1 us (6%)
  between operations  15.9 us (3%)
  starting transfers between devices  15.6 us (3%)
  other arithmetic  5.58 us (1%)
    all_gather x6, waiting for transfers between devices, all_rows(): lax.all_gather(for_sending(pair), 'mp', axis=0, tiled=True)  170 us
    all_to_all x3, blocking collectives, scatter_sum(): return jnp.sum(lax.all_to_all(chunks, axis, 0, 0, tiled=False), axis=0)  72.1 us
    ppermute x7, waiting for transfers between devices, per_device(): lax.ppermute(ring[-1], 'mp', [(dev, (dev + 1) % 8) for dev in range(8)])  50.7 us
    all_to_all x2, blocking collectives, gather_rows(): lax.all_to_all(jnp.broadcast_to(x[None], (count,) + x.shape), axis, 0, 0,...  46.8 us
    psum x1, blocking collectives, per_device(): lax.psum((jnp.sum(power_left * power_left), jnp.sum(power_right * power_r...  16.1 us
    all_gather x1, waiting for transfers between devices, per_device(): both_full = lax.all_gather(pieces, 'mp', axis=2, tiled=True)  15.1 us
    ppermute x7, starting transfers between devices, per_device(): lax.ppermute(ring[-1], 'mp', [(dev, (dev + 1) % 8) for dev in range(8)])  15.1 us
    unnamed x54, local copies, waits for them, and re-layouts  11 us
  transfers between devices with their start and end apart: 15, of which 13 were waited for; matrix products, arithmetic and copies ran while one was open for 8% of the time, Pallas kernels for 0%

profile of v1, /device:TPU:2, one launch (start us, length us, event | category | flops | bytes accessed | tf_op | source)
XLA Modules:
  0.0 465.3 jit_solution(16331814602641515880)
XLA Ops:
  7.2 1.4 bitcast_convert_fusion
  8.7 1.0 convert_reduce_fusion
  10.0 31.4 %all_to_all.25 = f32[64,12,96]{2,1,0:T(8,128)S(1)} all-to-all(f32[64,12,96]{2,1,0:T(8,128)S(1)} %reshape.45), channel_id=1, replica_groups=mesh['dp'=64,'mp'=8] {'dp'}, dimensions={0} | all-to-all | bytes 589824 | tf_op jit(solution)/shard_map/all_to_all | solution.py:43
  41.7 28.9 %all_to_all.26 = f32[64,2,12,96]{3,1,2,0:T(2,128)S(1)} all-to-all(f32[64,2,12,96]{3,1,2,0:T(2,128)S(1)} %broadcast_in_dim.4), channel_id=1, replica_groups=mesh['dp'=64,'mp'=8] {'dp'}, dimensions={0} | all-to-all | bytes 1179648 | tf_op jit(solution)/shard_map/all_to_all | solution.py:48
  70.6 1.1 copy.22
  71.8 3.5 collective-permute-start
  75.3 5.3 %collective-permute-done = bf16[768,96]{0,1:T(8,128)(2,1)S(1)} collective-permute-done((bf16[768,96]{0,1:T(8,128)(2,1)S(1)}, bf16[768,96]{0,1:T(8,128)(2,1)S(1)}, u32[]{:S(2)}, u32[]{:S(2)}) %collective-permute-start) | collective-permute-done | bytes 147488 | tf_op jit(solution)/shard_map/ppermute | solution.py:63
  80.5 1.9 collective-permute-start.1
  82.5 6.3 %collective-permute-done.1 = bf16[768,96]{0,1:T(8,128)(2,1)S(1)} collective-permute-done((bf16[768,96]{0,1:T(8,128)(2,1)S(1)}, bf16[768,96]{0,1:T(8,128)(2,1)S(1)}, u32[]{:S(2)}, u32[]{:S(2)}) %collective-permute-start.1) | collective-permute-done | bytes 147488 | tf_op jit(solution)/shard_map/ppermute | solution.py:63
  88.8 1.9 collective-permute-start.2
  90.7 6.3 %collective-permute-done.2 = bf16[768,96]{0,1:T(8,128)(2,1)S(1)} collective-permute-done((bf16[768,96]{0,1:T(8,128)(2,1)S(1)}, bf16[768,96]{0,1:T(8,128)(2,1)S(1)}, u32[]{:S(2)}, u32[]{:S(2)}) %collective-permute-start.2) | collective-permute-done | bytes 147488 | tf_op jit(solution)/shard_map/ppermute | solution.py:63
  97.0 1.9 collective-permute-start.3
  98.9 6.3 %collective-permute-done.3 = bf16[768,96]{0,1:T(8,128)(2,1)S(1)} collective-permute-done((bf16[768,96]{0,1:T(8,128)(2,1)S(1)}, bf16[768,96]{0,1:T(8,128)(2,1)S(1)}, u32[]{:S(2)}, u32[]{:S(2)}) %collective-permute-start.3) | collective-permute-done | bytes 147488 | tf_op jit(solution)/shard_map/ppermute | solution.py:63
  105.2 1.9 collective-permute-start.4
  107.2 6.3 %collective-permute-done.4 = bf16[768,96]{0,1:T(8,128)(2,1)S(1)} collective-permute-done((bf16[768,96]{0,1:T(8,128)(2,1)S(1)}, bf16[768,96]{0,1:T(8,128)(2,1)S(1)}, u32[]{:S(2)}, u32[]{:S(2)}) %collective-permute-start.4) | collective-permute-done | bytes 147488 | tf_op jit(solution)/shard_map/ppermute | solution.py:63
  113.5 1.9 collective-permute-start.5
  115.4 10.9 %collective-permute-done.5 = bf16[768,96]{0,1:T(8,128)(2,1)S(1)} collective-permute-done((bf16[768,96]{0,1:T(8,128)(2,1)S(1)}, bf16[768,96]{0,1:T(8,128)(2,1)S(1)}, u32[]{:S(2)}, u32[]{:S(2)}) %collective-permute-start.5) | collective-permute-done | bytes 147488 | tf_op jit(solution)/shard_map/ppermute | solution.py:63
  126.3 2.1 collective-permute-start.6
  128.4 9.2 %collective-permute-done.6 = bf16[768,96]{0,1:T(8,128)(2,1)S(1)} collective-permute-done((bf16[768,96]{0,1:T(8,128)(2,1)S(1)}, bf16[768,96]{0,1:T(8,128)(2,1)S(1)}, u32[]{:S(2)}, u32[]{:S(2)}) %collective-permute-start.6) | collective-permute-done | bytes 147488 | tf_op jit(solution)/shard_map/ppermute | solution.py:63
  140.3 0.7 constant_dynamic-update-slice_fusion.11
  148.4 3.2 reshape.52
  151.6 15.1 %all-gather.10.cloned.1.call-done = f32[2,768,768]{1,0,2:T(2,128)} async-done(((f32[2,768,96]{1,0,2:T(2,128)}), f32[2,768,768]{1,0,2:T(2,128)}) %all-gather.10.cloned.1.call-update) | async-done | bytes 4718608 | tf_op jit(solution)/shard_map/all_gather | solution.py:60
  166.8 9.3 %fusion.53 = (f32[1,768,768]{1,0,2:T(1,128)S(1)}, f32[1,768,768]{1,0,2:T(1,128)}) fusion(f32[2,768,768]{1,0,2:T(2,128)} %all-gather.10.cloned.1.call-done), kind=kLoop, calls=%fused_computation.87 | loop fusion | bytes 9437184 | tf_op jit(solution)/shard_map/slice | solution.py:67
  176.0 0.9 constant_dynamic-slice_fusion.1
  177.0 1.5 fusion.22
  178.6 2.4 fusion.19
  181.0 1.1 multiply_reduce_fusion.1
  182.1 3.1 multiply_reduce_fusion
  185.2 16.1 %all-reduce = (f32[]{:T(128)}, f32[]{:T(128)}) all-reduce(f32[]{:T(128)} %get-tuple-element.32, f32[]{:T(128)} %get-tuple-element.34), channel_id=1, replica_groups=mesh['dp'=64,'mp'=8] {'mp'}, use_global_device_ids=true, to_apply=%region_5.6 | all-reduce | flops 2 | bytes 16 | tf_op jit(solution)/shard_map/psum | solution.py:109
  202.0 0.7 multiply_convert_fusion.1
  203.5 1.6 multiply_convert_fusion
  205.2 37.3 %all-gather.12.cloned.1.call-done = bf16[768,768]{1,0:T(8,128)(2,1)} async-done(((bf16[96,768]{1,0:T(8,128)(2,1)}), bf16[768,768]{1,0:T(8,128)(2,1)}) %all-gather.12.cloned.1.call-update) | async-done | bytes 1179664 | tf_op jit(solution)/shard_map/all_gather | solution.py:29
  242.5 2.5 convolution_convert_fusion.3
  245.1 39.6 %all-gather.18.cloned.1.call-done = bf16[768,768]{1,0:T(8,128)(2,1)} async-done(((bf16[96,768]{1,0:T(8,128)(2,1)}), bf16[768,768]{1,0:T(8,128)(2,1)}) %all-gather.18.cloned.1.call-update) | async-done | bytes 1179664 | tf_op jit(solution)/shard_map/all_gather | solution.py:29
  284.7 2.5 convolution_convert_fusion.1
  287.3 40.1 %all-gather.14.cloned.1.call-done = bf16[768,768]{1,0:T(8,128)(2,1)} async-done(((bf16[96,768]{1,0:T(8,128)(2,1)}), bf16[768,768]{1,0:T(8,128)(2,1)}) %all-gather.14.cloned.1.call-update) | async-done | bytes 1179664 | tf_op jit(solution)/shard_map/all_gather | solution.py:29
  327.4 3.0 fusion.30
  330.7 2.0 fusion.4
  333.2 2.0 fusion.6
  335.2 34.4 %all-gather.20.cloned.1.call-done = bf16[768,768]{1,0:T(8,128)(2,1)} async-done(((bf16[96,768]{1,0:T(8,128)(2,1)}), bf16[768,768]{1,0:T(8,128)(2,1)}) %all-gather.20.cloned.1.call-update) | async-done | bytes 1179664 | tf_op jit(solution)/shard_map/all_gather | solution.py:29
  369.6 2.5 fusion.32
  372.9 12.5 %all_to_all.27 = f32[8,96,12]{1,2,0:T(8,128)S(1)} all-to-all(f32[8,96,12]{1,2,0:T(8,128)S(1)} %copy.23), channel_id=1, replica_groups=mesh['dp'=64,'mp'=8] {'mp'}, dimensions={0} | all-to-all | bytes 73728 | tf_op jit(solution)/shard_map/all_to_all | solution.py:43
  386.1 28.3 %all_to_all.28 = f32[64,12,96]{2,1,0:T(8,128)S(1)} all-to-all(f32[64,12,96]{2,1,0:T(8,128)S(1)} %reshape.48), channel_id=1, replica_groups=mesh['dp'=64,'mp'=8] {'dp'}, dimensions={0} | all-to-all | bytes 589824 | tf_op jit(solution)/shard_map/all_to_all | solution.py:43
  415.1 17.9 %all_to_all.29 = bf16[64,12,96]{2,1,0:T(8,128)(2,1)S(1)} all-to-all(bf16[64,12,96]{2,1,0:T(8,128)(2,1)S(1)} %broadcast_in_dim.5), channel_id=1, replica_groups=mesh['dp'=64,'mp'=8] {'dp'}, dimensions={0} | all-to-all | bytes 294912 | tf_op jit(solution)/shard_map/all_to_all | solution.py:48
  433.1 0.8 copy.26
  433.9 3.1 fusion.27
  437.0 18.4 %all-gather.22.cloned.1.call-done = bf16[768,768]{1,0:T(8,128)(2,1)} async-done(((bf16[96,768]{1,0:T(8,128)(2,1)}), bf16[768,768]{1,0:T(8,128)(2,1)}) %all-gather.22.cloned.1.call-update) | async-done | bytes 1179664 | tf_op jit(solution)/shard_map/all_gather | solution.py:29
  455.4 3.1 fusion.25
  (93 shorter events, 14.0 us)
Async XLA Ops:
  7.2 34.2 %copy-start.18 = (f32[12,96]{1,0:T(8,128)S(1)}, f32[12,96]{1,0:T(8,128)}, u32[]{:S(2)}) copy-start(f32[12,96]{1,0:T(8,128)} %param.10) | copy-start | bytes 13828
  7.2 141.3 %all-gather.24.cloned.1.call-start = ((), (), s32[]{:S(2)}) async-start(), calls=%async_computation.12 | async-start | bytes 1597440 | tf_op jit(solution)/shard_map/all_gather | solution.py:59
  8.7 158.1 %all-gather.10.cloned.1.call-start = ((), (), s32[]{:S(2)}) async-start(), calls=%async_computation.5 | async-start | bytes 5308416 | tf_op jit(solution)/shard_map/all_gather | solution.py:60
  41.3 30.5 %copy-start = (f32[768,96]{0,1:T(8,128)S(1)}, f32[768,96]{0,1:T(8,128)}, u32[]{:S(2)}) copy-start(f32[768,96]{0,1:T(8,128)} %param.13) | copy-start | bytes 884740
  41.4 30.4 %copy-start.15 = (f32[12,96]{1,0:T(8,128)}, f32[12,96]{1,0:T(8,128)S(1)}, u32[]{:S(2)}) copy-start(f32[12,96]{1,0:T(8,128)S(1)} %get-tuple-element.31) | copy-start | bytes 13828
  71.7 170.8 %all-gather.12.cloned.1.call-start = ((), (), s32[]{:S(2)}) async-start(), calls=%async_computation.6 | async-start | bytes 1327104 | tf_op jit(solution)/shard_map/all_gather | solution.py:29
  71.8 8.7 %collective-permute-start = (bf16[768,96]{0,1:T(8,128)(2,1)S(1)}, bf16[768,96]{0,1:T(8,128)(2,1)S(1)}, u32[]{:S(2)}, u32[]{:S(2)}) collective-permute-start(bf16[768,96]{0,1:T(8,128)(2,1)S(1)} %convert.2), channel_id=1, source_target_pairs={{0,1},{1,2},{2,3},{3,4},{4,5},{5,6},{6,7},{7,0},{8,9},{9,10},{10,1... | collective-permute-start | bytes 442376 | tf_op jit(solution)/shard_map/ppermute | solution.py:63
  80.5 8.2 %collective-permute-start.1 = (bf16[768,96]{0,1:T(8,128)(2,1)S(1)}, bf16[768,96]{0,1:T(8,128)(2,1)S(1)}, u32[]{:S(2)}, u32[]{:S(2)}) collective-permute-start(bf16[768,96]{0,1:T(8,128)(2,1)S(1)} %collective-permute-done), channel_id=1, source_target_pairs={{0,1},{1,2},{2,3},{3,4},{4,5},{5,6},{6,7},{7,0},{8,9},{9,10},{10,1... | collective-permute-start | bytes 442376 | tf_op jit(solution)/shard_map/ppermute | solution.py:63
  88.8 8.2 %collective-permute-start.2 = (bf16[768,96]{0,1:T(8,128)(2,1)S(1)}, bf16[768,96]{0,1:T(8,128)(2,1)S(1)}, u32[]{:S(2)}, u32[]{:S(2)}) collective-permute-start(bf16[768,96]{0,1:T(8,128)(2,1)S(1)} %collective-permute-done.1), channel_id=1, source_target_pairs={{0,1},{1,2},{2,3},{3,4},{4,5},{5,6},{6,7},{7,0},{8,9},{9,10},{10,1... | collective-permute-start | bytes 442376 | tf_op jit(solution)/shard_map/ppermute | solution.py:63
  97.0 8.2 %collective-permute-start.3 = (bf16[768,96]{0,1:T(8,128)(2,1)S(1)}, bf16[768,96]{0,1:T(8,128)(2,1)S(1)}, u32[]{:S(2)}, u32[]{:S(2)}) collective-permute-start(bf16[768,96]{0,1:T(8,128)(2,1)S(1)} %collective-permute-done.2), channel_id=1, source_target_pairs={{0,1},{1,2},{2,3},{3,4},{4,5},{5,6},{6,7},{7,0},{8,9},{9,10},{10,1... | collective-permute-start | bytes 442376 | tf_op jit(solution)/shard_map/ppermute | solution.py:63
  105.2 8.2 %collective-permute-start.4 = (bf16[768,96]{0,1:T(8,128)(2,1)S(1)}, bf16[768,96]{0,1:T(8,128)(2,1)S(1)}, u32[]{:S(2)}, u32[]{:S(2)}) collective-permute-start(bf16[768,96]{0,1:T(8,128)(2,1)S(1)} %collective-permute-done.3), channel_id=1, source_target_pairs={{0,1},{1,2},{2,3},{3,4},{4,5},{5,6},{6,7},{7,0},{8,9},{9,10},{10,1... | collective-permute-start | bytes 442376 | tf_op jit(solution)/shard_map/ppermute | solution.py:63
  113.5 12.8 %collective-permute-start.5 = (bf16[768,96]{0,1:T(8,128)(2,1)S(1)}, bf16[768,96]{0,1:T(8,128)(2,1)S(1)}, u32[]{:S(2)}, u32[]{:S(2)}) collective-permute-start(bf16[768,96]{0,1:T(8,128)(2,1)S(1)} %collective-permute-done.4), channel_id=1, source_target_pairs={{0,1},{1,2},{2,3},{3,4},{4,5},{5,6},{6,7},{7,0},{8,9},{9,10},{10,1... | collective-permute-start | bytes 442376 | tf_op jit(solution)/shard_map/ppermute | solution.py:63
  126.3 11.4 %collective-permute-start.6 = (bf16[768,96]{0,1:T(8,128)(2,1)S(1)}, bf16[768,96]{0,1:T(8,128)(2,1)S(1)}, u32[]{:S(2)}, u32[]{:S(2)}) collective-permute-start(bf16[768,96]{0,1:T(8,128)(2,1)S(1)} %collective-permute-done.5), channel_id=1, source_target_pairs={{0,1},{1,2},{2,3},{3,4},{4,5},{5,6},{6,7},{7,0},{8,9},{9,10},{10,1... | collective-permute-start | bytes 442376 | tf_op jit(solution)/shard_map/ppermute | solution.py:63
  151.6 25.4 %copy-start.12 = (f32[96,768]{1,0:T(8,128)S(1)}, f32[96,768]{1,0:T(8,128)}, u32[]{:S(2)}) copy-start(f32[96,768]{1,0:T(8,128)} %param.14) | copy-start | bytes 884740
  176.0 2.5 copy-start.13
  178.6 3.6 copy-start.9
  178.6 2.4 copy-start.3
  181.0 24.1 %copy-start.10 = (f32[96,768]{1,0:T(8,128)}, f32[96,768]{1,0:T(8,128)S(1)}, u32[]{:S(2)}) copy-start(f32[96,768]{1,0:T(8,128)S(1)} %fusion.19) | copy-start | bytes 884740
  202.7 124.7 %copy-start.5 = (bf16[96,768]{1,0:T(8,128)(2,1)S(1)}, bf16[96,768]{1,0:T(8,128)(2,1)}, u32[]{:S(2)}) copy-start(bf16[96,768]{1,0:T(8,128)(2,1)} %multiply_convert_fusion.1) | copy-start | bytes 442372
  202.7 81.9 %all-gather.18.cloned.1.call-start = ((), (), s32[]{:S(2)}) async-start(), calls=%async_computation.9 | async-start | bytes 1327104 | tf_op jit(solution)/shard_map/all_gather | solution.py:29
  205.1 122.3 %all-gather.14.cloned.1.call-start = ((), (), s32[]{:S(2)}) async-start(), calls=%async_computation.7 | async-start | bytes 1327104 | tf_op jit(solution)/shard_map/all_gather | solution.py:29
  245.0 85.7 %copy-start.11 = (f32[768,12]{0,1:T(8,128)S(1)}, f32[768,12]{0,1:T(8,128)}, u32[]{:S(2)}) copy-start(f32[768,12]{0,1:T(8,128)} %param.12) | copy-start | bytes 110596
  245.0 124.6 %all-gather.20.cloned.1.call-start = ((), (), s32[]{:S(2)}) async-start(), calls=%async_computation.10 | async-start | bytes 1327104 | tf_op jit(solution)/shard_map/all_gather | solution.py:29
  287.2 45.6 %copy-start.16 = (f32[12,96]{1,0:T(8,128)S(1)}, f32[12,96]{1,0:T(8,128)}, u32[]{:S(2)}) copy-start(f32[12,96]{1,0:T(8,128)} %param.11) | copy-start | bytes 13828
  287.2 146.6 %all-gather.16.cloned.1.call-start = ((), (), s32[]{:S(2)}) async-start(), calls=%async_computation.8 | async-start | bytes 1327104 | tf_op jit(solution)/shard_map/all_gather | solution.py:29
  330.4 39.2 %copy-start.4 = (bf16[96,768]{1,0:T(8,128)(2,1)S(1)}, bf16[96,768]{1,0:T(8,128)(2,1)}, u32[]{:S(2)}) copy-start(bf16[96,768]{1,0:T(8,128)(2,1)} %multiply_convert_fusion) | copy-start | bytes 442372
  330.4 39.2 %copy-start.8 = (bf16[96,768]{1,0:T(8,128)(2,1)S(1)}, bf16[96,768]{1,0:T(8,128)(2,1)}, u32[]{:S(2)}) copy-start(bf16[96,768]{1,0:T(8,128)(2,1)} %convolution_convert_fusion.1) | copy-start | bytes 442372
  330.4 124.9 %all-gather.22.cloned.1.call-start = ((), (), s32[]{:S(2)}) async-start(), calls=%async_computation.11 | async-start | bytes 1327104 | tf_op jit(solution)/shard_map/all_gather | solution.py:29
  330.7 2.4 copy-start.1
  332.8 36.8 %copy-start.2 = (bf16[768,768]{1,0:T(8,128)(2,1)S(1)}, bf16[768,768]{1,0:T(8,128)(2,1)}, u32[]{:S(2)}) copy-start(bf16[768,768]{1,0:T(8,128)(2,1)} %all-gather.18.cloned.1.call-done) | copy-start | bytes 3538948
  333.1 39.1 %copy-start.14 = (f32[12,96]{1,0:T(8,128)}, f32[12,96]{1,0:T(8,128)S(1)}, u32[]{:S(2)}) copy-start(f32[12,96]{1,0:T(8,128)S(1)} %fusion.46) | copy-start | bytes 13828
  372.2 42.2 %copy-start.17 = (f32[12,96]{1,0:T(8,128)S(1)}, f32[12,96]{1,0:T(8,128)}, u32[]{:S(2)}) copy-start(f32[12,96]{1,0:T(8,128)} %param.9) | copy-start | bytes 13828
  385.8 48.0 %copy-start.6 = (bf16[96,768]{1,0:T(8,128)(2,1)S(1)}, bf16[96,768]{1,0:T(8,128)(2,1)}, u32[]{:S(2)}) copy-start(bf16[96,768]{1,0:T(8,128)(2,1)} %fusion.30) | copy-start | bytes 442372
  414.3 41.0 %copy-start.7 = (bf16[96,768]{1,0:T(8,128)(2,1)S(1)}, bf16[96,768]{1,0:T(8,128)(2,1)}, u32[]{:S(2)}) copy-start(bf16[96,768]{1,0:T(8,128)(2,1)} %fusion.32) | copy-start | bytes 442372
Sparse Core Ops, SparseCore 0:
  11.9 87.7 all-gather.23
  101.8 64.9 all-gather.9
  202.8 39.5 all-gather.11
  244.4 40.2 all-gather.17
  287.2 40.2 all-gather.13
  329.3 40.2 all-gather.19
  372.2 40.2 all-gather.15
  415.1 40.1 all-gather.21
